TPU v7x, 256 devices: a whole 4x4x8 slice. The times are simulated.
256 devices in a mesh: dp: 64 (over x, z, core), tensor: 4 (over y).
Axes of the slice: x: 4, y: 4, z: 8, core: 2. Of those that a mesh axis runs over, the one named last changes fastest.
Arguments:
- tokens: bfloat16 [512, 16384], P('dp', 'tensor'), may hold values from -6 to 6
- clip_act: float32 [16384], P('tensor'), may hold values from 0.5 to 4
- weight: bfloat16 [16384, 49152], P('tensor', 'dp'), may hold values from -0.046875 to 0.046875
- clip_weight: float32 [49152], P('dp'), may hold values from 0.003 to 0.03
- cotangent: bfloat16 [512, 49152], P('tensor', 'dp'), may hold values from -16 to 16
Outputs:
- projected: bfloat16 [512, 49152], P('tensor', 'dp')
- token_grad: bfloat16 [512, 16384], P('dp', 'tensor')
- weight_grad: bfloat16 [16384, 49152], P('tensor', 'dp')
- clip_act_grad: float32 [16384], P('tensor')
- clip_weight_grad: float32 [49152], P('dp')
All inputs are finite; a program needn't handle non-finite values.
Results may differ from a plain program's by a relative error of at most 0.009.
Values may be sent and summed in bfloat16 or wider, within the bound.
No kernel may reach another device: no remote copies, remote signals or barrier semaphores. Data moves between devices by JAX's collectives and lax.ppermute only.
A program may use at most 128 MiB of HBM per device.

v0:
```python
import math
import jax
import jax.numpy as jnp
from jax import lax
from jax.sharding import PartitionSpec as P


def swapped(block, axis, bit):
    count = lax.axis_size(axis)
    route = []
    for low in range(count):
        high = low | 1 << bit
        if high != low and high < count:
            route += [(low, high), (high, low)]
    return lax.ppermute(block, axis, route)


def sylvester(order):
    index = lax.iota(jnp.int32, order)
    joined = jnp.bitwise_and(index[:, None], index[None, :])
    parity = jnp.zeros((order, order), jnp.int32)
    for bit_number in range(max(order.bit_length() - 1, 0)):
        parity = parity + jnp.bitwise_and(jnp.right_shift(joined, bit_number), 1)
    return (1 - 2 * jnp.bitwise_and(parity, 1)).astype(jnp.float32)


def local_rotate(values, norm_factor):
    row_total, width = values.shape
    levels = width.bit_length() - 1
    outer = 2 ** (levels // 2)
    inner = width // outer
    blocks = values.reshape(row_total, outer, inner)
    blocks = jnp.einsum("rab,ac->rcb", blocks, sylvester(outer), precision=lax.Precision.HIGHEST)
    blocks = jnp.einsum("rcb,bd->rcd", blocks, sylvester(inner), precision=lax.Precision.HIGHEST)
    return blocks.reshape(row_total, width) * norm_factor


def rotate(values):
    group_size = lax.axis_size("tensor")
    norm_factor = 1.0 / math.sqrt(values.shape[1] * group_size)
    mixed = local_rotate(values, norm_factor)
    position = lax.axis_index("tensor")
    for bit_number in range(group_size.bit_length() - 1):
        partner = swapped(mixed, "tensor", bit_number)
        upper = jnp.bitwise_and(jnp.right_shift(position, bit_number), 1) == 1
        mixed = jnp.where(upper, partner - mixed, mixed + partner)
    return mixed


def body(tokens, clip_act, weight, clip_weight, cotangent):
    rotated = rotate(tokens.astype(jnp.float32))
    ratio_act = rotated / clip_act
    tanh_act = jnp.tanh(ratio_act)
    quant_act = (clip_act * tanh_act).astype(jnp.bfloat16)
    slope_act = 1.0 - tanh_act * tanh_act
    edge_act = tanh_act - ratio_act * slope_act
    all_act = lax.all_gather(quant_act, "dp", axis=0, tiled=True)
    ratio_weight = weight.astype(jnp.float32) / clip_weight
    tanh_weight = jnp.tanh(ratio_weight)
    quant_weight = (clip_weight * tanh_weight).astype(jnp.bfloat16)
    block = all_act
    projected = lax.psum_scatter(
        jnp.dot(block, quant_weight, preferred_element_type=jnp.float32),
        "tensor",
        scatter_dimension=0,
        tiled=True,
    ).astype(jnp.bfloat16)
    all_cot = lax.all_gather(cotangent, "tensor", axis=0, tiled=True)
    weight_prod = lax.dot_general(
        all_act, all_cot, (((0,), (0,)), ((), ())), preferred_element_type=jnp.float32
    )
    slope_weight = 1.0 - tanh_weight * tanh_weight
    weight_grad = (weight_prod * slope_weight).astype(jnp.bfloat16)
    weight_terms = jnp.sum(weight_prod * (tanh_weight - ratio_weight * slope_weight), axis=0)
    clip_weight_grad = lax.psum(weight_terms, "tensor")
    block = all_cot
    act_prod = lax.psum_scatter(
        lax.dot_general(
            block, quant_weight, (((1,), (1,)), ((), ())), preferred_element_type=jnp.float32
        ),
        "dp",
        scatter_dimension=0,
        tiled=True,
    )
    clip_act_grad = lax.psum(jnp.sum(act_prod * edge_act, axis=0), "dp")
    pre_rotation = act_prod * slope_act
    token_grad = rotate(pre_rotation).astype(jnp.bfloat16)
    return (projected, token_grad, weight_grad, clip_act_grad, clip_weight_grad)


def solution(mesh):
    in_specs = (P("dp", "tensor"), P("tensor"), P("tensor", "dp"), P("dp"), P("tensor", "dp"))
    out_specs = (P("tensor", "dp"), P("dp", "tensor"), P("tensor", "dp"), P("tensor"), P("dp"))
    return jax.shard_map(body, mesh=mesh, in_specs=in_specs, out_specs=out_specs, check_vma=False)
```

profile of v0, /device:TPU:8, one launch (start us, length us, event | category | flops | bytes accessed | tf_op | source)
XLA Modules:
  0.0 489.3 jit_solution(6198169342169980642)
XLA Ops:
  7.2 0.0 reduce-scatter.7.cloned.1.call-start
  7.2 14.6 %all_gather.7 = bf16[512,768]{1,0:T(8,128)(2,1)S(1)} all-gather(bf16[128,768]{1,0:T(8,128)(2,1)} %param.9), channel_id=1, replica_groups=mesh['dp'=64,'tensor'=4] {'tensor'}, dimensions={0}, use_global_device_ids=true | all-gather | bytes 983040 | tf_op jit(solution)/shard_map/all_gather | solution.py:68
  21.8 9.5 %convolution_bitcast_fusion = f32[512,4096]{0,1:T(8,128)} fusion(bf16[512,768]{1,0:T(8,128)(2,1)S(1)} %all_gather.7, f32[768]{0:T(1024)} %param.8, bf16[4096,768]{1,0:T(8,128)(2,1)} %param.7), kind=kOutput, calls=%fused_computation.5 | convolution fusion | flops 3233808384 | bytes 15469568 | tf_op jit(solution)/shard_map/dot_general | solution.py:78
  31.3 8.9 %copy.19 = f32[512,4096]{1,0:T(8,128)} copy(f32[512,4096]{0,1:T(8,128)} %convolution_bitcast_fusion) | data formatting | bytes 16777216
  40.2 0.0 reduce-scatter.7.cloned.1.call-update
  40.2 0.0 all-gather.2.cloned.1.call-start
  40.3 0.8 copy-done
  41.1 0.2 reshape.24
  41.2 0.3 convolution_bitcast_fusion.2
  41.6 0.4 convolution_multiply_fusion.1
  42.0 0.1 mul.67
  42.1 2.0 collective-permute-start
  44.1 3.8 collective-permute-done
  47.9 2.7 collective-permute-start.1
  50.6 3.9 collective-permute-done.1
  54.5 140.9 %reduce-scatter.7.cloned.1.call-done = f32[8,4096]{1,0:T(8,128)} async-done(((f32[512,4096]{1,0:T(8,128)}), f32[8,4096]{1,0:T(8,128)}) %reduce-scatter.7.cloned.1.call-update) | async-done | bytes 131088 | tf_op jit(solution)/shard_map/reduce_scatter | solution.py:77
  195.4 1.0 multiply_reduce_fusion.1
  196.4 1.6 fusion
  197.9 0.0 all-gather.2.cloned.1.call-update
  198.0 0.0 reduce-scatter.5.cloned.1.call-start
  198.0 0.1 reshape.25
  198.1 0.4 convolution_bitcast_fusion.1
  198.5 0.4 convolution_multiply_fusion
  198.9 0.1 mul.74
  199.1 0.6 collective-permute-start.2
  199.7 246.6 %psum.14 = f32[4096]{0:T(1024)} all-reduce(f32[4096]{0:T(1024)S(1)} %get-tuple-element.10), channel_id=1, replica_groups=mesh['dp'=64,'tensor'=4] {'dp'}, use_global_device_ids=true, to_apply=%region_3.4 | all-reduce | flops 4096 | bytes 32768 | tf_op jit(solution)/shard_map/psum | solution.py:85
  446.2 2.6 collective-permute-start.3
  448.9 8.7 %fusion.33 = f32[512,768]{1,0:T(8,128)} fusion(bf16[512,4096]{1,0:T(8,128)(2,1)} %all-gather.2.cloned.1.call-done, f32[768]{0:T(1024)S(1)} %copy-done.2, bf16[4096,768]{1,0:T(8,128)(2,1)} %param.7), kind=kOutput, calls=%fused_computation.51 | convolution fusion | flops 3233808384 | bytes 12061696 | tf_op jit(solution)/shard_map/dot_general | solution.py:63
  457.6 0.7 select_convert_fusion
  458.3 12.4 %multiply_reduce_fusion = (f32[768]{0:T(1024)S(1)}, bf16[4096,768]{1,0:T(8,128)(2,1)}) fusion(f32[768]{0:T(1024)S(1)} %copy-done.2, bf16[4096,768]{1,0:T(8,128)(2,1)} %param.7, bf16[512,4096]{1,0:T(8,128)(2,1)} %all-gather.2.cloned.1.call-done, bf16[512,768]{1,0:T(8,128)(2,1)S(1)} %all_gather.7), kind=kOutput, calls=%fused_computation | convolution fusion | flops 3252681984 | bytes 17569792 | tf_op jit(solution)/shard_map/dot_general | solution.py:69
  470.7 10.4 %psum.15 = f32[768]{0:T(1024)} all-reduce(f32[768]{0:T(1024)S(1)} %get-tuple-element.12), channel_id=1, replica_groups=mesh['dp'=64,'tensor'=4] {'tensor'}, use_global_device_ids=true, to_apply=%region_5.6 | all-reduce | flops 768 | bytes 6144 | tf_op jit(solution)/shard_map/psum | solution.py:75
  481.1 1.7 convert_element_type.35
  (12 shorter events, 0.1 us)
Async XLA Ops:
  7.2 188.2 %reduce-scatter.7.cloned.1.call-start = ((), (), s32[]{:S(2)}) async-start(), calls=%async_computation.4 | async-start | bytes 8519680 | tf_op jit(solution)/shard_map/reduce_scatter | solution.py:77
  40.2 0.8 copy-start
  40.2 155.2 %copy-start.1 = (f32[4096]{0:T(1024)S(1)}, f32[4096]{0:T(1024)}, u32[]{:S(2)}) copy-start(f32[4096]{0:T(1024)} %param.6) | copy-start | bytes 49156
  40.2 408.7 %copy-start.2 = (f32[768]{0:T(1024)S(1)}, f32[768]{0:T(1024)}, u32[]{:S(2)}) copy-start(f32[768]{0:T(1024)} %param.8) | copy-start | bytes 9220
  40.2 408.6 %all-gather.2.cloned.1.call-start = ((), (), s32[]{:S(2)}) async-start(), calls=%async_computation.2 | async-start | bytes 4259840 | tf_op jit(solution)/shard_map/all_gather | solution.py:57
  42.1 5.8 %collective-permute-start = (f32[8,4096]{1,0:T(8,128)S(1)}, f32[8,4096]{1,0:T(8,128)S(1)}, u32[]{:S(2)}, u32[]{:S(2)}) collective-permute-start(f32[8,4096]{1,0:T(8,128)S(1)} %mul.67), channel_id=1, source_target_pairs={{0,1},{1,0},{2,3},{3,2},{4,5},{5,4},{6,7},{7,6},{8,9},{9,8},{10,11... | collective-permute-start | bytes 393224 | tf_op jit(solution)/shard_map/ppermute | solution.py:15
  47.9 6.6 %collective-permute-start.1 = (f32[8,4096]{1,0:T(8,128)S(1)}, f32[8,4096]{1,0:T(8,128)S(1)}, u32[]{:S(2)}, u32[]{:S(2)}) collective-permute-start(f32[8,4096]{1,0:T(8,128)S(1)} %add_select_fusion.1), channel_id=1, source_target_pairs={{0,2},{2,0},{1,3},{3,1},{4,6},{6,4},{5,7},{7,5},{8,10},{10,8},{9,1... | collective-permute-start | bytes 393224 | tf_op jit(solution)/shard_map/ppermute | solution.py:15
  198.0 283.1 %reduce-scatter.5.cloned.1.call-start = ((), (), s32[]{:S(2)}) async-start(), calls=%async_computation.3 | async-start | bytes 1966080 | tf_op jit(solution)/shard_map/reduce_scatter | solution.py:62
  199.1 247.2 %collective-permute-start.2 = (f32[8,4096]{1,0:T(8,128)S(1)}, f32[8,4096]{1,0:T(8,128)S(1)}, u32[]{:S(2)}, u32[]{:S(2)}) collective-permute-start(f32[8,4096]{1,0:T(8,128)S(1)} %mul.74), channel_id=1, source_target_pairs={{0,1},{1,0},{2,3},{3,2},{4,5},{5,4},{6,7},{7,6},{8,9},{9,8},{10,11... | collective-permute-start | bytes 393224 | tf_op jit(solution)/shard_map/ppermute | solution.py:15
  446.2 11.4 %collective-permute-start.3 = (f32[8,4096]{1,0:T(8,128)S(1)}, f32[8,4096]{1,0:T(8,128)S(1)}, u32[]{:S(2)}, u32[]{:S(2)}) collective-permute-start(f32[8,4096]{1,0:T(8,128)S(1)} %add_select_fusion), channel_id=1, source_target_pairs={{0,2},{2,0},{1,3},{3,1},{4,6},{6,4},{5,7},{7,5},{8,10},{10,8},{9,1... | collective-permute-start | bytes 393224 | tf_op jit(solution)/shard_map/ppermute | solution.py:15
Sparse Core Ops, SparseCore 0:
  40.4 154.9 reduce-scatter.6
  198.7 77.4 all-gather.1
  457.7 19.8 reduce-scatter.4
where the time goes:
time: 490 us; the launch traced here: 489 us
  blocking collectives  271 us (55%)
  waiting for transfers between devices  149 us (30%)
  matrix products  32.2 us (7%)
  between operations  13.8 us (3%)
  local copies, waits for them, and re-layouts  10.2 us (2%)
  starting transfers between devices  8.06 us (2%)
  other arithmetic  4.94 us (1%)
    psum x1, blocking collectives, body(): clip_act_grad = lax.psum(jnp.sum(act_prod * edge_act, axis=0), 'dp')  247 us
    reduce_scatter x1, waiting for transfers between devices, body(): lax.psum_scatter(lax.dot_general(block, quant_weight, (((1,), (1,)), ((),...  141 us
    all_gather x1, blocking collectives, body(): all_cot = lax.all_gather(cotangent, 'tensor', axis=0, tiled=True)  14.6 us
    dot_general x1, matrix products, body(): lax.dot_general(all_act, all_cot, (((0,), (0,)), ((), ())), preferred_ele...  12.4 us
    psum x1, blocking collectives, body(): clip_weight_grad = lax.psum(weight_terms, 'tensor')  10.4 us
  transfers between devices with their start and end apart: 7, of which 3 were waited for; matrix products, arithmetic and copies ran while one was open for 5% of the time, Pallas kernels for 0%

commit v1 on v0

--- a/solution.py
+++ b/solution.py
@@ -3,6 +3,7 @@
 import jax.numpy as jnp
 from jax import lax
 from jax.sharding import PartitionSpec as P
+from jax.lax import all_to_all, axis_size
 
 
 def swapped(block, axis, bit):
@@ -65,7 +66,12 @@
         scatter_dimension=0,
         tiled=True,
     ).astype(jnp.bfloat16)
-    all_cot = lax.all_gather(cotangent, "tensor", axis=0, tiled=True)
+    items = []
+    for _ in range(axis_size("tensor")):
+        items.append(cotangent)
+    everything = jnp.stack(items, axis=0)
+    u_next = all_to_all(everything, axis_name="tensor", split_axis=0, concat_axis=0)
+    all_cot = jnp.concatenate(u_next, axis=0)
     weight_prod = lax.dot_general(
         all_act, all_cot, (((0,), (0,)), ((), ())), preferred_element_type=jnp.float32
     )

time: 490 us -> 491 us (level)
    all_to_all x0 -> x1, blocking collectives: none -> 15.5 us  [body(): all_to_all(everything, axis_name='tensor', split_axis=0, concat_axis=0)]
    all_gather x1 -> x0, blocking collectives: 14.6 us -> none  [body(): all_cot = lax.all_gather(cotangent, 'tensor', axis=0, tiled=True)]
where the time goes in v1:
time: 491 us
  blocking collectives  272 us (55%)
  waiting for transfers between devices  149 us (30%)
  matrix products  32.2 us (7%)
  between operations  13.8 us (3%)
  local copies, waits for them, and re-layouts  11.2 us (2%)
  starting transfers between devices  6.52 us (1%)
  other arithmetic  4.94 us (1%)
    psum x1, blocking collectives, body(): clip_act_grad = lax.psum(jnp.sum(act_prod * edge_act, axis=0), 'dp')  247 us
    reduce_scatter x1, waiting for transfers between devices, body(): lax.psum_scatter(lax.dot_general(block, quant_weight, (((1,), (1,)), ((),...  141 us
    all_to_all x1, blocking collectives, body(): all_to_all(everything, axis_name='tensor', split_axis=0, concat_axis=0)  15.5 us
    dot_general x1, matrix products, body(): lax.dot_general(all_act, all_cot, (((0,), (0,)), ((), ())), preferred_ele...  12.4 us
    psum x1, blocking collectives, body(): clip_weight_grad = lax.psum(weight_terms, 'tensor')  10.3 us
  transfers between devices with their start and end apart: 7, of which 3 were waited for; matrix products, arithmetic and copies ran while one was open for 5% of the time, Pallas kernels for 0%

profile of v1, /device:TPU:8, one launch (start us, length us, event | category | flops | bytes accessed | tf_op | source)
XLA Modules:
  0.0 490.5 jit_solution(15147431979704995441)
XLA Ops:
  7.2 0.0 reduce-scatter.7.cloned.1.call-start
  7.2 1.0 stack.2
  8.2 15.5 %all_to_all.5 = bf16[4,128,768]{2,1,0:T(8,128)(2,1)S(1)} all-to-all(bf16[4,128,768]{2,1,0:T(8,128)(2,1)S(1)} %stack.2), channel_id=1, replica_groups=mesh['dp'=64,'tensor'=4] {'tensor'}, dimensions={0} | all-to-all | bytes 1572864 | tf_op jit(solution)/shard_map/all_to_all | solution.py:73
  23.7 9.5 %convolution_bitcast_fusion = f32[512,4096]{0,1:T(8,128)} fusion(bf16[512,768]{1,0:T(8,128)(2,1)S(1)} %bitcast.25, f32[768]{0:T(1024)} %param.8, bf16[4096,768]{1,0:T(8,128)(2,1)} %param.7), kind=kOutput, calls=%fused_computation.5 | convolution fusion | flops 3233808384 | bytes 15469568 | tf_op jit(solution)/shard_map/dot_general | solution.py:84
  33.2 8.9 %copy.19 = f32[512,4096]{1,0:T(8,128)} copy(f32[512,4096]{0,1:T(8,128)} %convolution_bitcast_fusion) | data formatting | bytes 16777216
  42.2 0.0 reduce-scatter.7.cloned.1.call-update
  42.2 0.0 all-gather.2.cloned.1.call-start
  42.2 0.8 copy-done
  43.0 0.2 reshape.29
  43.2 0.3 convolution_bitcast_fusion.2
  43.5 0.4 convolution_multiply_fusion.1
  43.9 0.1 mul.67
  44.0 1.5 collective-permute-start
  45.6 3.5 collective-permute-done
  49.1 1.6 collective-permute-start.1
  50.7 5.0 %collective-permute-done.1 = f32[8,4096]{1,0:T(8,128)S(1)} collective-permute-done((f32[8,4096]{1,0:T(8,128)S(1)}, f32[8,4096]{1,0:T(8,128)S(1)}, u32[]{:S(2)}, u32[]{:S(2)}) %collective-permute-start.1) | collective-permute-done | bytes 131104 | tf_op jit(solution)/shard_map/ppermute | solution.py:16
  55.7 140.9 %reduce-scatter.7.cloned.1.call-done = f32[8,4096]{1,0:T(8,128)} async-done(((f32[512,4096]{1,0:T(8,128)}), f32[8,4096]{1,0:T(8,128)}) %reduce-scatter.7.cloned.1.call-update) | async-done | bytes 131088 | tf_op jit(solution)/shard_map/reduce_scatter | solution.py:83
  196.6 1.0 multiply_reduce_fusion.1
  197.6 1.6 fusion
  199.2 0.0 reduce-scatter.5.cloned.1.call-start
  199.2 0.1 reshape.31
  199.3 0.4 convolution_bitcast_fusion.1
  199.8 0.4 convolution_multiply_fusion
  200.2 0.1 mul.74
  200.3 0.6 collective-permute-start.2
  200.9 246.5 %psum.14 = f32[4096]{0:T(1024)} all-reduce(f32[4096]{0:T(1024)S(1)} %get-tuple-element.10), channel_id=1, replica_groups=mesh['dp'=64,'tensor'=4] {'dp'}, use_global_device_ids=true, to_apply=%region_3.4 | all-reduce | flops 4096 | bytes 32768 | tf_op jit(solution)/shard_map/psum | solution.py:91
  447.4 2.7 collective-permute-start.3
  450.1 8.7 %fusion.33 = f32[512,768]{1,0:T(8,128)} fusion(bf16[512,4096]{1,0:T(8,128)(2,1)} %all-gather.2.cloned.1.call-done, f32[768]{0:T(1024)S(1)} %copy-done.2, bf16[4096,768]{1,0:T(8,128)(2,1)} %param.7), kind=kOutput, calls=%fused_computation.51 | convolution fusion | flops 3233808384 | bytes 12061696 | tf_op jit(solution)/shard_map/dot_general | solution.py:64
  458.9 0.7 select_convert_fusion
  459.5 12.4 %multiply_reduce_fusion = (f32[768]{0:T(1024)S(1)}, bf16[4096,768]{1,0:T(8,128)(2,1)}) fusion(f32[768]{0:T(1024)S(1)} %copy-done.2, bf16[4096,768]{1,0:T(8,128)(2,1)} %param.7, bf16[512,4096]{1,0:T(8,128)(2,1)} %all-gather.2.cloned.1.call-done, bf16[512,768]{1,0:T(8,128)(2,1)S(1)} %bitcast.26), kind=kOutput, calls=%fused_computation | convolution fusion | flops 3252681984 | bytes 17569792 | tf_op jit(solution)/shard_map/dot_general | solution.py:75
  472.0 10.3 %psum.15 = f32[768]{0:T(1024)} all-reduce(f32[768]{0:T(1024)S(1)} %get-tuple-element.12), channel_id=1, replica_groups=mesh['dp'=64,'tensor'=4] {'tensor'}, use_global_device_ids=true, to_apply=%region_5.6 | all-reduce | flops 768 | bytes 6144 | tf_op jit(solution)/shard_map/psum | solution.py:81
  482.3 1.7 convert_element_type.35
  (13 shorter events, 0.1 us)
Async XLA Ops:
  7.2 189.4 %reduce-scatter.7.cloned.1.call-start = ((), (), s32[]{:S(2)}) async-start(), calls=%async_computation.5 | async-start | bytes 8519680 | tf_op jit(solution)/shard_map/reduce_scatter | solution.py:83
  42.2 0.8 copy-start
  42.2 154.4 %copy-start.1 = (f32[4096]{0:T(1024)S(1)}, f32[4096]{0:T(1024)}, u32[]{:S(2)}) copy-start(f32[4096]{0:T(1024)} %param.6) | copy-start | bytes 49156
  42.2 408.0 %copy-start.2 = (f32[768]{0:T(1024)S(1)}, f32[768]{0:T(1024)}, u32[]{:S(2)}) copy-start(f32[768]{0:T(1024)} %param.8) | copy-start | bytes 9220
  42.2 407.9 %all-gather.2.cloned.1.call-start = ((), (), s32[]{:S(2)}) async-start(), calls=%async_computation.3 | async-start | bytes 4259840 | tf_op jit(solution)/shard_map/all_gather | solution.py:58
  44.0 5.1 %collective-permute-start = (f32[8,4096]{1,0:T(8,128)S(1)}, f32[8,4096]{1,0:T(8,128)S(1)}, u32[]{:S(2)}, u32[]{:S(2)}) collective-permute-start(f32[8,4096]{1,0:T(8,128)S(1)} %mul.67), channel_id=1, source_target_pairs={{0,1},{1,0},{2,3},{3,2},{4,5},{5,4},{6,7},{7,6},{8,9},{9,8},{10,11... | collective-permute-start | bytes 393224 | tf_op jit(solution)/shard_map/ppermute | solution.py:16
  49.1 6.6 %collective-permute-start.1 = (f32[8,4096]{1,0:T(8,128)S(1)}, f32[8,4096]{1,0:T(8,128)S(1)}, u32[]{:S(2)}, u32[]{:S(2)}) collective-permute-start(f32[8,4096]{1,0:T(8,128)S(1)} %add_select_fusion.1), channel_id=1, source_target_pairs={{0,2},{2,0},{1,3},{3,1},{4,6},{6,4},{5,7},{7,5},{8,10},{10,8},{9,1... | collective-permute-start | bytes 393224 | tf_op jit(solution)/shard_map/ppermute | solution.py:16
  199.2 283.1 %reduce-scatter.5.cloned.1.call-start = ((), (), s32[]{:S(2)}) async-start(), calls=%async_computation.4 | async-start | bytes 1966080 | tf_op jit(solution)/shard_map/reduce_scatter | solution.py:63
  200.3 247.1 %collective-permute-start.2 = (f32[8,4096]{1,0:T(8,128)S(1)}, f32[8,4096]{1,0:T(8,128)S(1)}, u32[]{:S(2)}, u32[]{:S(2)}) collective-permute-start(f32[8,4096]{1,0:T(8,128)S(1)} %mul.74), channel_id=1, source_target_pairs={{0,1},{1,0},{2,3},{3,2},{4,5},{5,4},{6,7},{7,6},{8,9},{9,8},{10,11... | collective-permute-start | bytes 393224 | tf_op jit(solution)/shard_map/ppermute | solution.py:16
  447.4 11.4 %collective-permute-start.3 = (f32[8,4096]{1,0:T(8,128)S(1)}, f32[8,4096]{1,0:T(8,128)S(1)}, u32[]{:S(2)}, u32[]{:S(2)}) collective-permute-start(f32[8,4096]{1,0:T(8,128)S(1)} %add_select_fusion), channel_id=1, source_target_pairs={{0,2},{2,0},{1,3},{3,1},{4,6},{6,4},{5,7},{7,5},{8,10},{10,8},{9,1... | collective-permute-start | bytes 393224 | tf_op jit(solution)/shard_map/ppermute | solution.py:16
Sparse Core Ops, SparseCore 0:
  42.3 154.2 reduce-scatter.6
  199.9 77.4 all-gather.1
  459.0 19.8 reduce-scatter.4
